TPU v7x, 32 devices: a whole 2x2x4 slice. The times are simulated.
32 devices in a mesh: ctx: 4 (over y, x), pair: 4 (over z), dp: 2 (over core).
Axes of the slice: x: 2, y: 2, z: 4, core: 2. Of those that a mesh axis runs over, the one named last changes fastest.
Arguments:
- queries: bfloat16 [8, 4, 128, 2048], P(('dp', 'ctx'), 'pair'), parts along dimension 0, may hold values from -8 to 8
- resp_keys: bfloat16 [8, 4, 128, 1024], P(('dp', 'ctx'), 'pair'), parts along dimension 0, may hold values from -6 to 6
- resp_values: bfloat16 [8, 4, 128, 1024], P(('dp', 'ctx'), 'pair'), parts along dimension 0, may hold values from -6 to 6
- d_out: bfloat16 [8, 4, 128, 2048], P(('dp', 'ctx'), 'pair'), parts along dimension 0, may hold values from -6 to 6
- prefix_kv: bfloat16 [4, 512, 2, 1024], P('dp', 'ctx', None, 'pair'), parts along dimension 0, may hold values from -8 to 8
- prefix_blocks: int32 [8, 4, 4], P(('dp', 'ctx'), 'pair'), parts along dimension 0, may hold values 0 or 1
- resp_lengths: int32 [8, 4], P(('dp', 'ctx'), 'pair'), parts along dimension 0, may hold values from 32 to 128, as said below
- pair_prompt: int32 [8], P('dp'), parts along dimension 0, may hold values from 0 to 1, as said below
Outputs:
- d_queries: bfloat16 [8, 4, 128, 2048], P(('dp', 'ctx'), 'pair'), parts along dimension 0
- d_resp_keys: bfloat16 [8, 4, 128, 1024], P(('dp', 'ctx'), 'pair'), parts along dimension 0
- d_resp_values: bfloat16 [8, 4, 128, 1024], P(('dp', 'ctx'), 'pair'), parts along dimension 0
- d_prefix: float32 [4, 512, 2, 1024], P('dp', 'ctx', None, 'pair'), parts along dimension 0
There are 2 independent parts, one for each index of `dp`. A program takes and returns all parts, laid end to end along the dimension named above; each array names one. Nothing has to cross between parts.
Inputs may be any that keep to these rules, and one draw needn't show every extreme that they name: `pair_prompt`: each prompt is answered by exactly two indices of pair, one chosen and one rejected response. `resp_lengths`: some response fills all 128 slots.
All inputs are finite; a program needn't handle non-finite values. No bound on the sum of `prefix_blocks` on one device may be relied on, other than what follows from the above.
Results may differ from a plain program's by a relative error of at most 0.012.
The roundings to bfloat16 on the way count: a program that leaves them out, or rounds other values in their place, can miss the bound.
Values may be sent and summed in bfloat16 or wider, within the bound.
No kernel may reach another device: no remote copies, remote signals or barrier semaphores. Data moves between devices by JAX's collectives and lax.ppermute only.
A program may use at most 128 MiB of HBM per device.

v0:
```python
import jax
import jax.numpy as jnp
from jax import lax
from jax.sharding import PartitionSpec as P

KV_HEADS = 8
GROUP = 2
HEAD_DIM = 128
BLOCK = 128
scale_factor = 144.0 ** (-0.5)
neg_big = -1e30


def gather_rows(kv_part):
    return lax.all_gather(kv_part, "ctx", axis=1, tiled=True)


def pick_prompt(kv_part, pair_prompt):
    outgoing = jnp.take(kv_part, pair_prompt, axis=0)
    return lax.all_to_all(outgoing, "pair", split_axis=0, concat_axis=3, tiled=True)


def shards(
    queries, resp_keys, resp_values, d_out, prefix_kv, prefix_blocks, resp_lengths, pair_prompt
):
    prefix_panel = gather_rows(pick_prompt(prefix_kv, pair_prompt))
    prefix_panel = prefix_panel[0]
    resp_rows = queries.shape[2]
    pre_rows = prefix_panel.shape[0]
    n_prompts = prefix_kv.shape[0]
    all_rows = pre_rows + resp_rows
    keys_heads = jnp.transpose(
        jnp.concatenate([prefix_panel[:, 0], resp_keys[0, 0]], 0).reshape(
            all_rows, KV_HEADS, HEAD_DIM
        ),
        (1, 0, 2),
    )
    values_heads = jnp.transpose(
        jnp.concatenate([prefix_panel[:, 1], resp_values[0, 0]], 0).reshape(
            all_rows, KV_HEADS, HEAD_DIM
        ),
        (1, 0, 2),
    )
    query_heads = jnp.transpose(
        queries[0, 0].reshape(resp_rows, KV_HEADS, GROUP, HEAD_DIM), (1, 2, 0, 3)
    )
    positions = jnp.arange(resp_rows, dtype=jnp.int32)
    live_rows = positions < resp_lengths[0, 0]
    grad_rows = jnp.where(live_rows[:, None], d_out[0, 0], jnp.zeros_like(d_out[0, 0]))
    grad_heads = jnp.transpose(
        grad_rows.reshape(resp_rows, KV_HEADS, GROUP, HEAD_DIM), (1, 2, 0, 3)
    )
    visible = prefix_blocks[0, 0] > 0
    prefix_mask = jnp.broadcast_to(visible[:, None], (pre_rows // BLOCK, BLOCK)).reshape(pre_rows)
    causal = positions[:, None] >= positions[None, :]
    allowed = jnp.concatenate(
        [jnp.broadcast_to(prefix_mask[None, :], (resp_rows, pre_rows)), causal], 1
    )

    def one_head(items):
        key_rows, value_rows, query_rows, grad_part = items
        scores = (
            jnp.einsum("jqd,kd->jqk", query_rows, key_rows, preferred_element_type=jnp.float32)
            * scale_factor
        )
        scores = jnp.where(allowed[None], scores, neg_big)
        row_peak = jnp.max(scores, axis=-1, keepdims=True)
        raised = jnp.exp(scores - row_peak)
        weights = raised / jnp.sum(raised, axis=-1, keepdims=True)
        probs_low = weights.astype(jnp.bfloat16)
        attended = jnp.einsum(
            "jqk,kd->jqd", probs_low, value_rows, preferred_element_type=jnp.float32
        )
        attended = lax.optimization_barrier(attended.astype(jnp.bfloat16)).astype(jnp.float32)
        row_delta = jnp.sum(grad_part.astype(jnp.float32) * attended, axis=-1)
        d_probs = jnp.einsum(
            "jqd,kd->jqk", grad_part, value_rows, preferred_element_type=jnp.float32
        )
        ds_low = (weights * (d_probs - row_delta[..., None])).astype(jnp.bfloat16)
        query_grad = (
            jnp.einsum("jqk,kd->jqd", ds_low, key_rows, preferred_element_type=jnp.float32)
            * scale_factor
        )
        key_grad = (
            jnp.einsum("jqk,jqd->kd", ds_low, query_rows, preferred_element_type=jnp.float32)
            * scale_factor
        )
        value_grad = jnp.einsum(
            "jqk,jqd->kd", probs_low, grad_part, preferred_element_type=jnp.float32
        )
        both_grads = jnp.stack([key_grad, value_grad], 1).astype(jnp.bfloat16)
        return (query_grad.astype(jnp.bfloat16), both_grads)

    query_grads, kv_grads = lax.map(one_head, (keys_heads, values_heads, query_heads, grad_heads))
    d_queries = jnp.transpose(query_grads, (2, 0, 1, 3)).reshape(1, 1, resp_rows, -1)
    own_grads = jnp.transpose(kv_grads[:, pre_rows:], (1, 2, 0, 3)).reshape(resp_rows, 2, -1)
    d_resp_keys = own_grads[:, 0].reshape(1, 1, resp_rows, -1)
    d_resp_values = own_grads[:, 1].reshape(1, 1, resp_rows, -1)
    prefix_part = jnp.transpose(kv_grads[:, :pre_rows], (1, 2, 0, 3)).reshape(1, pre_rows, 2, -1)
    pieces = lax.all_to_all(prefix_part, "ctx", split_axis=1, concat_axis=0, tiled=True)
    ctx_total = jnp.sum(pieces.astype(jnp.float32), axis=0).astype(jnp.bfloat16)
    arrived = lax.all_to_all(ctx_total[None], "pair", split_axis=3, concat_axis=0, tiled=True)
    prompt_hits = (pair_prompt[:, None] == jnp.arange(n_prompts, dtype=jnp.int32)[None, :]).astype(
        jnp.float32
    )
    d_prefix = jnp.sum(
        prompt_hits[:, :, None, None, None] * arrived.astype(jnp.float32)[:, None], axis=0
    )
    return (d_queries, d_resp_keys, d_resp_values, d_prefix)


def solution(mesh):
    placed = (
        P(("dp", "ctx"), "pair", None, None),
        P(("dp", "ctx"), "pair", None, None),
        P(("dp", "ctx"), "pair", None, None),
        P(("dp", "ctx"), "pair", None, None),
        P("dp", "ctx", None, "pair"),
        P(("dp", "ctx"), "pair", None),
        P(("dp", "ctx"), "pair"),
        P("dp"),
    )
    return jax.shard_map(
        shards,
        mesh=mesh,
        in_specs=placed,
        out_specs=(
            P(("dp", "ctx"), "pair", None, None),
            P(("dp", "ctx"), "pair", None, None),
            P(("dp", "ctx"), "pair", None, None),
            P("dp", "ctx", None, "pair"),
        ),
        check_vma=False,
    )
```

profile of v0, /device:TPU:0, one launch (start us, length us, event | category | flops | bytes accessed | tf_op | source)
XLA Modules:
  0.0 192.6 jit_solution(804473975615161115)
XLA Ops:
  8.6 1.6 gather_fusion
  10.8 20.7 %all_to_all.39 = bf16[4,128,2,256]{3,2,1,0:T(2,128)(2,1)S(1)} all-to-all(bf16[4,128,2,256]{3,2,1,0:T(2,128)(2,1)S(1)} %broadcast_select_fusion), channel_id=1, replica_groups=mesh['ctx'=4,'pair'=4,'dp'=2] {'pair'}, dimensions={0} | all-to-all | bytes 1048576 | tf_op jit(solution)/shard_map/all_to_all | solution.py:20
  35.3 31.8 %all-gather.2.cloned.1.call-done = bf16[1,512,2,1024]{1,3,2,0:T(8,128)(2,1)} async-done(((bf16[1,128,2,1024]{1,3,2,0:T(8,128)(2,1)}), bf16[1,512,2,1024]{1,3,2,0:T(8,128)(2,1)}) %all-gather.2.cloned.1.call-update) | async-done | bytes 2097168 | tf_op jit(solution)/shard_map/all_gather | solution.py:15
  67.1 1.7 fusion.55
  70.1 50.9 %while.12 = (s32[]{:T(128)}, bf16[8,2,128,128]{3,2,1,0:T(8,128)(2,1)}, bf16[8,640,2,128]{3,1,2,0:T(8,128)(2,1)}, pred[128,640]{1,0:T(8,128)(4,1)S(1)}, bf16[8,2,...) while((s32[]{:T(128)}, ...), condition=%wide.region_4.5_spmd, body=%wide.region_0.4_spmd.sunk | while | flops 254427520 | bytes 6446201 | solution.py:94
  73.3 1.8 fusion.93
  79.6 1.8 fusion.93
  86.0 1.8 fusion.93
  89.1 1.4 fusion.90
  92.4 1.8 fusion.93
  98.7 1.8 fusion.93
  105.1 1.8 fusion.93
  108.2 1.4 fusion.90
  111.4 1.8 fusion.93
  114.6 1.4 fusion.90
  117.8 1.8 fusion.93
  121.0 3.2 %copy.93 = bf16[8,640,2,128]{1,3,0,2:T(8,128)(2,1)S(1)} copy(bf16[8,640,2,128]{3,1,2,0:T(8,128)(2,1)} %get-tuple-element.48) | data formatting | bytes 5242880 | tf_op jit(solution)/shard_map/while | solution.py:94
  124.1 1.5 slice.30
  125.7 6.2 %copy.94 = bf16[1,512,2,1024]{3,2,0,1:T(2,128)(2,1)} copy(bf16[1,512,2,1024]{1,3,2,0:T(8,128)(2,1)} %bitcast.153) | data formatting | bytes 4194304 | tf_op jit(solution)/shard_map/reshape | solution.py:99
  131.9 29.2 %all_to_all.40 = bf16[1,512,2,1024]{3,2,0,1:T(2,128)(2,1)S(1)} all-to-all(bf16[1,512,2,1024]{3,2,0,1:T(2,128)(2,1)} %copy.94), channel_id=1, replica_groups=mesh['ctx'=4,'pair'=4,'dp'=2] {'ctx'}, dimensions={1} | all-to-all | bytes 4194304 | tf_op jit(solution)/shard_map/all_to_all | solution.py:100
  161.1 3.1 %reduce_sum.39 = bf16[128,2,1024]{2,1,0:T(2,128)(2,1)S(1)} reduce(bf16[4,128,2,1024]{3,2,1,0:T(2,128)(2,1)S(1)} %bitcast.152, bf16[]{:T(256)} %constant.29.clone.1), dimensions={0}, to_apply=%region_5.6 | reduce | flops 786432 | bytes 2621442 | tf_op jit(solution)/shard_map/reduce_sum | solution.py:101
  164.2 1.9 copy.95
  166.1 4.6 %all-to-all-start.2 = ((bf16[1,128,2,1024]{1,2,0,3:T(2,128)(2,1)}), bf16[1,128,2,1024]{1,2,0,3:T(2,128)(2,1)S(1)}, u32[]{:S(2)}, u32[]{:S(2)}) async-start(bf16[1,128,2,1024]{1,2,0,3:T(2,128)(2,1)} %copy.95), calls=%async_computation.2 | async-start | bytes 1048576 | tf_op jit(solution)/shard_map/all_to_all | solution.py:102
  174.5 9.3 %all-to-all-done.2 = bf16[1,128,2,1024]{1,2,0,3:T(2,128)(2,1)S(1)} async-done(((bf16[1,128,2,1024]{1,2,0,3:T(2,128)(2,1)}), bf16[1,128,2,1024]{1,2,0,3:T(2,128)(2,1)S(1)}, u32[]{:S(2)}, u32[]{:S(2)}) %all-to-all-start.2) | async-done | bytes 524320 | tf_op jit(solution)/shard_map/all_to_all | solution.py:102
  (124 shorter events, 43.8 us)
Async XLA Ops:
  7.2 1.4 copy-start
  7.2 59.9 %all-gather.2.cloned.1.call-start = ((), (), s32[]{:S(2)}) async-start(), calls=%async_computation.3 | async-start | bytes 2621440 | tf_op jit(solution)/shard_map/all_gather | solution.py:15
  10.2 22.4 %copy-start.1 = (bf16[1,1,128,2048]{3,2,1,0:T(8,128)(2,1)S(1)}, bf16[1,1,128,2048]{3,2,1,0:T(8,128)(2,1)}, u32[]{:S(2)}) copy-start(bf16[1,1,128,2048]{3,2,1,0:T(8,128)(2,1)} %param.10) | copy-start | bytes 1572868
  10.7 22.2 %copy-start.4 = (bf16[1,1,128,1024]{3,2,1,0:T(8,128)(2,1)S(1)}, bf16[1,1,128,1024]{3,2,1,0:T(8,128)(2,1)}, u32[]{:S(2)}) copy-start(bf16[1,1,128,1024]{3,2,1,0:T(8,128)(2,1)} %param.11) | copy-start | bytes 786436
  10.8 22.4 %copy-start.5 = (bf16[1,1,128,1024]{3,2,1,0:T(8,128)(2,1)S(1)}, bf16[1,1,128,1024]{3,2,1,0:T(8,128)(2,1)}, u32[]{:S(2)}) copy-start(bf16[1,1,128,1024]{3,2,1,0:T(8,128)(2,1)} %param.12) | copy-start | bytes 786436
  31.5 1.8 copy-start.2
  32.6 1.6 copy-start.7
  161.1 9.6 %copy-start.6 = (s32[4]{0:T(128)S(1)}, s32[4]{0:T(128)}, u32[]{:S(2)}) copy-start(s32[4]{0:T(128)} %param.17) | copy-start | bytes 52
  161.1 9.7 %copy-start.3 = (bf16[8,2,128,128]{3,2,1,0:T(8,128)(2,1)S(1)}, bf16[8,2,128,128]{3,2,1,0:T(8,128)(2,1)}, u32[]{:S(2)}) copy-start(bf16[8,2,128,128]{3,2,1,0:T(8,128)(2,1)} %get-tuple-element.47) | copy-start | bytes 1572868
  166.1 17.7 %all-to-all-start.2 = ((bf16[1,128,2,1024]{1,2,0,3:T(2,128)(2,1)}), bf16[1,128,2,1024]{1,2,0,3:T(2,128)(2,1)S(1)}, u32[]{:S(2)}, u32[]{:S(2)}) async-start(bf16[1,128,2,1024]{1,2,0,3:T(2,128)(2,1)} %copy.95), calls=%async_computation.2 | async-start | bytes 1048576 | tf_op jit(solution)/shard_map/all_to_all | solution.py:102
Sparse Core Ops, SparseCore 0:
  32.7 34.2 all-gather.1
where the time goes:
time: 194 us; the launch traced here: 193 us
  blocking collectives  50 us (26%)
  waiting for transfers between devices  41.1 us (21%)
  matrix products  34.8 us (18%)
  local copies, waits for them, and re-layouts  31.2 us (16%)
  other arithmetic  15.5 us (8%)
  between operations  14.9 us (8%)
  starting transfers between devices  4.64 us (2%)
    all_gather x1, waiting for transfers between devices, gather_rows(): return lax.all_gather(kv_part, 'ctx', axis=1, tiled=True)  31.8 us
    all_to_all x1, blocking collectives, shards(): lax.all_to_all(prefix_part, 'ctx', split_axis=1, concat_axis=0, tiled=True)  29.2 us
    all_to_all x1, blocking collectives, pick_prompt(): lax.all_to_all(outgoing, 'pair', split_axis=0, concat_axis=3, tiled=True)  20.7 us
    dot_general x8, matrix products, one_head(): jnp.einsum('jqk,kd->jqd', ds_low, key_rows, preferred_element_type=jnp.fl...  14.4 us
    sub x8, matrix products, one_head(): raised = jnp.exp(scores - row_peak)  11.3 us
    all_to_all x1, waiting for transfers between devices, shards(): lax.all_to_all(ctx_total[None], 'pair', split_axis=3, concat_axis=0, tile...  9.32 us
    dynamic_slice x16, local copies, waits for them, and re-layouts, shards(): lax.map(one_head, (keys_heads, values_heads, query_heads, grad_heads))  7.76 us
    reshape x1, local copies, waits for them, and re-layouts, shards(): jnp.transpose(kv_grads[:, :pre_rows], (1, 2, 0, 3))  6.24 us
  transfers between devices with their start and end apart: 2, of which 2 were waited for; matrix products, arithmetic and copies ran while one was open for 3% of the time, Pallas kernels for 0%

commit v1 on v0

--- a/solution.py
+++ b/solution.py
@@ -11,8 +11,24 @@
 neg_big = -1e30
 
 
+def gather_around(x, axis, dim):
+    ways, here, step = (lax.axis_size(axis), lax.axis_index(axis), x.shape[dim])
+    shape = [n * ways if d == dim else n for d, n in enumerate(x.shape)]
+    full = lax.dynamic_update_slice_in_dim(jnp.zeros(shape, x.dtype), x, here * step, axis=dim)
+    going_up = going_down = x
+    for far in range(1, ways // 2 + 1):
+        going_up = lax.ppermute(going_up, axis, [(d, (d + 1) % ways) for d in range(ways)])
+        full = lax.dynamic_update_slice_in_dim(full, going_up, (here - far) % ways * step, axis=dim)
+        if 2 * far < ways:
+            going_down = lax.ppermute(going_down, axis, [(d, (d - 1) % ways) for d in range(ways)])
+            full = lax.dynamic_update_slice_in_dim(
+                full, going_down, (here + far) % ways * step, axis=dim
+            )
+    return full
+
+
 def gather_rows(kv_part):
-    return lax.all_gather(kv_part, "ctx", axis=1, tiled=True)
+    return gather_around(kv_part, "ctx", 1)
 
 
 def pick_prompt(kv_part, pair_prompt):

time: 194 us -> 177 us (0.912)
  blocking collectives: 50 us -> 27.5 us
  between operations: 14.9 us -> 1.55 us
  waiting for transfers between devices: 41.1 us -> 51 us
  starting transfers between devices: 4.64 us -> 13.5 us
    all_gather x1 -> x0, waiting for transfers between devices: 31.8 us -> none  [gather_rows(): return lax.all_gather(kv_part, 'ctx', axis=1, tiled=True)]
    ppermute x0 -> x3, waiting for transfers between devices: none -> 29.3 us  [the longest x2 20.2 us: gather_around(): lax.ppermute(going_up, axis, [(d, (d + 1) % ways) for d in range(ways)])]
    all_to_all x1 -> x0, blocking collectives: 20.7 us -> none  [pick_prompt(): lax.all_to_all(outgoing, 'pair', split_axis=0, concat_axis=3, tiled=True)]
    all_to_all x0 -> x1, waiting for transfers between devices: none -> 13.7 us  [pick_prompt(): lax.all_to_all(outgoing, 'pair', split_axis=0, concat_axis=3, tiled=True)]
    all_to_all x0 -> x1, starting transfers between devices: none -> 6.45 us  [pick_prompt(): lax.all_to_all(outgoing, 'pair', split_axis=0, concat_axis=3, tiled=True)]
    ppermute x0 -> x3, starting transfers between devices: none -> 3.57 us  [the longest x2 2.14 us: gather_around(): lax.ppermute(going_up, axis, [(d, (d + 1) % ways) for d in range(ways)])]
  transfers between devices with their start and end apart: 2 -> 5, of which waited for: 2 -> 5; matrix products, arithmetic and copies ran while one was open for 3% -> 4% of each run, Pallas kernels for 0% -> 0%
where the time goes in v1:
time: 177 us; the launch traced here: 176 us
  waiting for transfers between devices  51 us (29%)
  matrix products  34.8 us (20%)
  local copies, waits for them, and re-layouts  30.7 us (17%)
  blocking collectives  27.5 us (16%)
  other arithmetic  16.3 us (9%)
  starting transfers between devices  13.5 us (8%)
    all_to_all x1, blocking collectives, shards(): lax.all_to_all(prefix_part, 'ctx', split_axis=1, concat_axis=0, tiled=True)  27.5 us
    ppermute x2, waiting for transfers between devices, gather_around(): lax.ppermute(going_up, axis, [(d, (d + 1) % ways) for d in range(ways)])  20.2 us
    dot_general x8, matrix products, one_head(): jnp.einsum('jqk,kd->jqd', ds_low, key_rows, preferred_element_type=jnp.fl...  14.4 us
    all_to_all x1, waiting for transfers between devices, pick_prompt(): lax.all_to_all(outgoing, 'pair', split_axis=0, concat_axis=3, tiled=True)  13.7 us
    sub x8, matrix products, one_head(): raised = jnp.exp(scores - row_peak)  11.3 us
    ppermute x1, waiting for transfers between devices, gather_around(): lax.ppermute(going_down, axis, [(d, (d - 1) % ways) for d in range(ways)])  9.14 us
    all_to_all x1, waiting for transfers between devices, shards(): lax.all_to_all(ctx_total[None], 'pair', split_axis=3, concat_axis=0, tile...  8 us
    dynamic_slice x16, local copies, waits for them, and re-layouts, shards(): lax.map(one_head, (keys_heads, values_heads, query_heads, grad_heads))  7.75 us
  transfers between devices with their start and end apart: 5, of which 5 were waited for; matrix products, arithmetic and copies ran while one was open for 4% of the time, Pallas kernels for 0%

profile of v1, /device:TPU:0, one launch (start us, length us, event | category | flops | bytes accessed | tf_op | source)
XLA Modules:
  0.0 175.8 jit_solution(16630813539073967170)
XLA Ops:
  2.0 1.6 gather_fusion
  5.0 6.4 %all-to-all-start = ((bf16[4,128,2,256]{3,2,1,0:T(2,128)(2,1)}), bf16[4,128,2,256]{3,2,1,0:T(2,128)(2,1)S(1)}, u32[]{:S(2)}, u32[]{:S(2)}) async-start(bf16[4,128,2,256]{3,2,1,0:T(2,128)(2,1)} %broadcast_select_fusion), calls=%async_computation | async-start | bytes 1048576 | tf_op jit(solution)/shard_map/all_to_all | solution.py:36
  12.2 13.7 %all-to-all-done = bf16[4,128,2,256]{3,2,1,0:T(2,128)(2,1)S(1)} async-done(((bf16[4,128,2,256]{3,2,1,0:T(2,128)(2,1)}), bf16[4,128,2,256]{3,2,1,0:T(2,128)(2,1)S(1)}, u32[]{:S(2)}, u32[]{:S(2)}) %all-to-all-start) | async-done | bytes 524320 | tf_op jit(solution)/shard_map/all_to_all | solution.py:36
  26.4 1.5 collective-permute-start
  31.2 11.1 %collective-permute-done = bf16[1,128,2,1024]{1,3,2,0:T(8,128)(2,1)} collective-permute-done((bf16[1,128,2,1024]{1,3,2,0:T(8,128)(2,1)S(1)}, bf16[1,128,2,1024]{1,3,2,0:T(8,128)(2,1)}, u32[]{:S(2)}, u32[]{:S(2)}) %collective-permute-start) | collective-permute-done | bytes 524320 | tf_op jit(solution)/shard_map/ppermute | solution.py:20
  44.4 9.1 %collective-permute-done.1 = bf16[1,128,2,1024]{1,3,2,0:T(8,128)(2,1)S(1)} collective-permute-done((bf16[1,128,2,1024]{1,3,2,0:T(8,128)(2,1)S(1)}, bf16[1,128,2,1024]{1,3,2,0:T(8,128)(2,1)S(1)}, u32[]{:S(2)}, u32[]{:S(2)}) %collective-permute-start.1) | collective-permute-done | bytes 524320 | tf_op jit(solution)/shard_map/ppermute | solution.py:23
  53.6 9.1 %collective-permute-done.2 = bf16[1,128,2,1024]{1,3,2,0:T(8,128)(2,1)S(1)} collective-permute-done((bf16[1,128,2,1024]{1,3,2,0:T(8,128)(2,1)}, bf16[1,128,2,1024]{1,3,2,0:T(8,128)(2,1)S(1)}, u32[]{:S(2)}, u32[]{:S(2)}) %collective-permute-start.2) | collective-permute-done | bytes 524320 | tf_op jit(solution)/shard_map/ppermute | solution.py:20
  64.3 50.9 %while.12 = (s32[]{:T(128)}, bf16[8,2,128,128]{3,2,1,0:T(8,128)(2,1)}, bf16[8,640,2,128]{3,1,2,0:T(8,128)(2,1)}, pred[128,640]{1,0:T(8,128)(4,1)S(1)}, bf16[8,2,...) while((s32[]{:T(128)}, ...), condition=%wide.region_4.5_spmd, body=%wide.region_0.4_spmd.sunk | while | flops 254427520 | bytes 6446201 | solution.py:110
  67.5 1.8 %fusion.93 = bf16[8,2,128,128]{3,2,1,0:T(8,128)(2,1)} fusion(bf16[8,2,128,128]{3,2,1,0:T(8,128)(2,1)} %get-tuple-element.180, s32[]{:T(128)S(6)} %copy.122, bf16[2,128,640]{2,1,0:T(8,128)(2,1)S(1)} %fusion.92, bf16[8,640,128]{1,2,0:T(8,128)(2,1)} %get-tuple-element.193), kind=kOutput, calls=%fused_computation.20.clone.1 | convolution fusion | flops 42008576 | bytes 558080 | tf_op jit(solution)/shard_map/while/body/eval_jaxpr/jqk,kd->jqd/dot_general | solution.py:97
  73.9 1.8 %fusion.93 = bf16[8,2,128,128]{3,2,1,0:T(8,128)(2,1)} fusion(bf16[8,2,128,128]{3,2,1,0:T(8,128)(2,1)} %get-tuple-element.180, s32[]{:T(128)S(6)} %copy.122, bf16[2,128,640]{2,1,0:T(8,128)(2,1)S(1)} %fusion.92, bf16[8,640,128]{1,2,0:T(8,128)(2,1)} %get-tuple-element.193), kind=kOutput, calls=%fused_computation.20.clone.1 | convolution fusion | flops 42008576 | bytes 558080 | tf_op jit(solution)/shard_map/while/body/eval_jaxpr/jqk,kd->jqd/dot_general | solution.py:97
  80.2 1.8 %fusion.93 = bf16[8,2,128,128]{3,2,1,0:T(8,128)(2,1)} fusion(bf16[8,2,128,128]{3,2,1,0:T(8,128)(2,1)} %get-tuple-element.180, s32[]{:T(128)S(6)} %copy.122, bf16[2,128,640]{2,1,0:T(8,128)(2,1)S(1)} %fusion.92, bf16[8,640,128]{1,2,0:T(8,128)(2,1)} %get-tuple-element.193), kind=kOutput, calls=%fused_computation.20.clone.1 | convolution fusion | flops 42008576 | bytes 558080 | tf_op jit(solution)/shard_map/while/body/eval_jaxpr/jqk,kd->jqd/dot_general | solution.py:97
  86.6 1.8 %fusion.93 = bf16[8,2,128,128]{3,2,1,0:T(8,128)(2,1)} fusion(bf16[8,2,128,128]{3,2,1,0:T(8,128)(2,1)} %get-tuple-element.180, s32[]{:T(128)S(6)} %copy.122, bf16[2,128,640]{2,1,0:T(8,128)(2,1)S(1)} %fusion.92, bf16[8,640,128]{1,2,0:T(8,128)(2,1)} %get-tuple-element.193), kind=kOutput, calls=%fused_computation.20.clone.1 | convolution fusion | flops 42008576 | bytes 558080 | tf_op jit(solution)/shard_map/while/body/eval_jaxpr/jqk,kd->jqd/dot_general | solution.py:97
  92.9 1.8 %fusion.93 = bf16[8,2,128,128]{3,2,1,0:T(8,128)(2,1)} fusion(bf16[8,2,128,128]{3,2,1,0:T(8,128)(2,1)} %get-tuple-element.180, s32[]{:T(128)S(6)} %copy.122, bf16[2,128,640]{2,1,0:T(8,128)(2,1)S(1)} %fusion.92, bf16[8,640,128]{1,2,0:T(8,128)(2,1)} %get-tuple-element.193), kind=kOutput, calls=%fused_computation.20.clone.1 | convolution fusion | flops 42008576 | bytes 558080 | tf_op jit(solution)/shard_map/while/body/eval_jaxpr/jqk,kd->jqd/dot_general | solution.py:97
  99.3 1.8 %fusion.93 = bf16[8,2,128,128]{3,2,1,0:T(8,128)(2,1)} fusion(bf16[8,2,128,128]{3,2,1,0:T(8,128)(2,1)} %get-tuple-element.180, s32[]{:T(128)S(6)} %copy.122, bf16[2,128,640]{2,1,0:T(8,128)(2,1)S(1)} %fusion.92, bf16[8,640,128]{1,2,0:T(8,128)(2,1)} %get-tuple-element.193), kind=kOutput, calls=%fused_computation.20.clone.1 | convolution fusion | flops 42008576 | bytes 558080 | tf_op jit(solution)/shard_map/while/body/eval_jaxpr/jqk,kd->jqd/dot_general | solution.py:97
  105.6 1.8 %fusion.93 = bf16[8,2,128,128]{3,2,1,0:T(8,128)(2,1)} fusion(bf16[8,2,128,128]{3,2,1,0:T(8,128)(2,1)} %get-tuple-element.180, s32[]{:T(128)S(6)} %copy.122, bf16[2,128,640]{2,1,0:T(8,128)(2,1)S(1)} %fusion.92, bf16[8,640,128]{1,2,0:T(8,128)(2,1)} %get-tuple-element.193), kind=kOutput, calls=%fused_computation.20.clone.1 | convolution fusion | flops 42008576 | bytes 558080 | tf_op jit(solution)/shard_map/while/body/eval_jaxpr/jqk,kd->jqd/dot_general | solution.py:97
  112.0 1.8 %fusion.93 = bf16[8,2,128,128]{3,2,1,0:T(8,128)(2,1)} fusion(bf16[8,2,128,128]{3,2,1,0:T(8,128)(2,1)} %get-tuple-element.180, s32[]{:T(128)S(6)} %copy.122, bf16[2,128,640]{2,1,0:T(8,128)(2,1)S(1)} %fusion.92, bf16[8,640,128]{1,2,0:T(8,128)(2,1)} %get-tuple-element.193), kind=kOutput, calls=%fused_computation.20.clone.1 | convolution fusion | flops 42008576 | bytes 558080 | tf_op jit(solution)/shard_map/while/body/eval_jaxpr/jqk,kd->jqd/dot_general | solution.py:97
  115.2 3.2 %copy.97 = bf16[8,640,2,128]{1,3,0,2:T(8,128)(2,1)S(1)} copy(bf16[8,640,2,128]{3,1,2,0:T(8,128)(2,1)} %get-tuple-element.48) | data formatting | bytes 5242880 | tf_op jit(solution)/shard_map/while | solution.py:110
  118.4 1.5 slice.30
  119.9 6.3 %copy.98 = bf16[1,512,2,1024]{3,2,0,1:T(2,128)(2,1)} copy(bf16[1,512,2,1024]{1,3,2,0:T(8,128)(2,1)} %bitcast.159) | data formatting | bytes 4194304 | tf_op jit(solution)/shard_map/reshape | solution.py:115
  126.2 27.5 %all_to_all.39 = bf16[1,512,2,1024]{3,2,0,1:T(2,128)(2,1)S(1)} all-to-all(bf16[1,512,2,1024]{3,2,0,1:T(2,128)(2,1)} %copy.98), channel_id=1, replica_groups=mesh['ctx'=4,'pair'=4,'dp'=2] {'ctx'}, dimensions={1} | all-to-all | bytes 4194304 | tf_op jit(solution)/shard_map/all_to_all | solution.py:116
  153.7 3.1 %reduce_sum.39 = bf16[128,2,1024]{2,1,0:T(2,128)(2,1)S(1)} reduce(bf16[4,128,2,1024]{3,2,1,0:T(2,128)(2,1)S(1)} %bitcast.158, bf16[]{:T(256)} %constant.78.clone.1), dimensions={0}, to_apply=%region_5.6 | reduce | flops 786432 | bytes 2621442 | tf_op jit(solution)/shard_map/reduce_sum | solution.py:117
  156.8 1.9 %copy.99 = bf16[1,128,2,1024]{1,2,0,3:T(2,128)(2,1)} copy(bf16[1,128,2,1024]{3,2,1,0:T(2,128)(2,1)S(1)} %bitcast.168) | data formatting | bytes 1048576 | tf_op jit(solution)/shard_map/broadcast_in_dim | solution.py:118
  158.7 3.5 %all-to-all-start.2 = ((bf16[1,128,2,1024]{1,2,0,3:T(2,128)(2,1)}), bf16[1,128,2,1024]{1,2,0,3:T(2,128)(2,1)S(1)}, u32[]{:S(2)}, u32[]{:S(2)}) async-start(bf16[1,128,2,1024]{1,2,0,3:T(2,128)(2,1)} %copy.99), calls=%async_computation.2 | async-start | bytes 1048576 | tf_op jit(solution)/shard_map/all_to_all | solution.py:118
  165.9 8.0 %all-to-all-done.2 = bf16[1,128,2,1024]{1,2,0,3:T(2,128)(2,1)S(1)} async-done(((bf16[1,128,2,1024]{1,2,0,3:T(2,128)(2,1)}), bf16[1,128,2,1024]{1,2,0,3:T(2,128)(2,1)S(1)}, u32[]{:S(2)}, u32[]{:S(2)}) %all-to-all-start.2) | async-done | bytes 524320 | tf_op jit(solution)/shard_map/all_to_all | solution.py:118
  (133 shorter events, 51.9 us)
Async XLA Ops:
  0.6 1.4 copy-start
  0.6 11.5 %copy-start.7 = (s32[1,1,4]{2,1,0:T(1,128)S(1)}, s32[1,1,4]{2,1,0:T(1,128)}, u32[]{:S(2)}) copy-start(s32[1,1,4]{2,1,0:T(1,128)} %param.15) | copy-start | bytes 52
  2.0 25.9 %copy-start.1 = (bf16[1,1,128,2048]{3,2,1,0:T(8,128)(2,1)S(1)}, bf16[1,1,128,2048]{3,2,1,0:T(8,128)(2,1)}, u32[]{:S(2)}) copy-start(bf16[1,1,128,2048]{3,2,1,0:T(8,128)(2,1)} %param.10) | copy-start | bytes 1572868
  3.7 24.6 %copy-start.4 = (bf16[1,1,128,1024]{3,2,1,0:T(8,128)(2,1)S(1)}, bf16[1,1,128,1024]{3,2,1,0:T(8,128)(2,1)}, u32[]{:S(2)}) copy-start(bf16[1,1,128,1024]{3,2,1,0:T(8,128)(2,1)} %param.11) | copy-start | bytes 786436
  5.0 23.4 %copy-start.5 = (bf16[1,1,128,1024]{3,2,1,0:T(8,128)(2,1)S(1)}, bf16[1,1,128,1024]{3,2,1,0:T(8,128)(2,1)}, u32[]{:S(2)}) copy-start(bf16[1,1,128,1024]{3,2,1,0:T(8,128)(2,1)} %param.12) | copy-start | bytes 786436
  5.0 23.6 %copy-start.2 = (bf16[1,1,128,2048]{3,2,1,0:T(8,128)(2,1)S(1)}, bf16[1,1,128,2048]{3,2,1,0:T(8,128)(2,1)}, u32[]{:S(2)}) copy-start(bf16[1,1,128,2048]{3,2,1,0:T(8,128)(2,1)} %param.13) | copy-start | bytes 1572868
  5.0 20.9 %all-to-all-start = ((bf16[4,128,2,256]{3,2,1,0:T(2,128)(2,1)}), bf16[4,128,2,256]{3,2,1,0:T(2,128)(2,1)S(1)}, u32[]{:S(2)}, u32[]{:S(2)}) async-start(bf16[4,128,2,256]{3,2,1,0:T(2,128)(2,1)} %broadcast_select_fusion), calls=%async_computation | async-start | bytes 1048576 | tf_op jit(solution)/shard_map/all_to_all | solution.py:36
  26.4 15.9 %collective-permute-start = (bf16[1,128,2,1024]{1,3,2,0:T(8,128)(2,1)S(1)}, bf16[1,128,2,1024]{1,3,2,0:T(8,128)(2,1)}, u32[]{:S(2)}, u32[]{:S(2)}) collective-permute-start(bf16[1,128,2,1024]{1,3,2,0:T(8,128)(2,1)S(1)} %bitcast.163), channel_id=1, source_target_pairs={{0,8},{8,16},{16,24},{24,0},{1,9},{9,17},{17,25},{25,1},{2,10},{10... | collective-permute-start | bytes 1572872 | tf_op jit(solution)/shard_map/ppermute | solution.py:20
  29.7 23.8 %collective-permute-start.1 = (bf16[1,128,2,1024]{1,3,2,0:T(8,128)(2,1)S(1)}, bf16[1,128,2,1024]{1,3,2,0:T(8,128)(2,1)S(1)}, u32[]{:S(2)}, u32[]{:S(2)}) collective-permute-start(bf16[1,128,2,1024]{1,3,2,0:T(8,128)(2,1)S(1)} %bitcast.164), channel_id=1, source_target_pairs={{0,24},{8,0},{16,8},{24,16},{1,25},{9,1},{17,9},{25,17},{2,26},{10... | collective-permute-start | bytes 1572872 | tf_op jit(solution)/shard_map/ppermute | solution.py:23
  42.3 20.4 %collective-permute-start.2 = (bf16[1,128,2,1024]{1,3,2,0:T(8,128)(2,1)}, bf16[1,128,2,1024]{1,3,2,0:T(8,128)(2,1)S(1)}, u32[]{:S(2)}, u32[]{:S(2)}) collective-permute-start(bf16[1,128,2,1024]{1,3,2,0:T(8,128)(2,1)} %collective-permute-done), channel_id=1, source_target_pairs={{0,8},{8,16},{16,24},{24,0},{1,9},{9,17},{17,25},{25,1},{2,10},{10... | collective-permute-start | bytes 1572872 | tf_op jit(solution)/shard_map/ppermute | solution.py:20
  153.7 8.5 %copy-start.6 = (s32[4]{0:T(128)S(1)}, s32[4]{0:T(128)}, u32[]{:S(2)}) copy-start(s32[4]{0:T(128)} %param.17) | copy-start | bytes 52
  153.7 8.5 %copy-start.3 = (bf16[8,2,128,128]{3,2,1,0:T(8,128)(2,1)S(1)}, bf16[8,2,128,128]{3,2,1,0:T(8,128)(2,1)}, u32[]{:S(2)}) copy-start(bf16[8,2,128,128]{3,2,1,0:T(8,128)(2,1)} %get-tuple-element.47) | copy-start | bytes 1572868
  158.7 15.2 %all-to-all-start.2 = ((bf16[1,128,2,1024]{1,2,0,3:T(2,128)(2,1)}), bf16[1,128,2,1024]{1,2,0,3:T(2,128)(2,1)S(1)}, u32[]{:S(2)}, u32[]{:S(2)}) async-start(bf16[1,128,2,1024]{1,2,0,3:T(2,128)(2,1)} %copy.99), calls=%async_computation.2 | async-start | bytes 1048576 | tf_op jit(solution)/shard_map/all_to_all | solution.py:118
